TPU v7x, 32 devices: a whole 2x2x4 slice. The times are simulated.
32 devices in a mesh: cand: 4 (over y, x), hist: 8 (over z, core).
Axes of the slice: x: 2, y: 2, z: 4, core: 2. Of those that a mesh axis runs over, the one named last changes fastest.
Arguments:
- cand_x: bfloat16 [2, 1024, 1024], P(None, ('cand', 'hist')), may hold values from -6 to 6
- qu_weight: bfloat16 [1024, 2048], replicated, may hold values from -0.1875 to 0.1875
- out_weight: bfloat16 [1024, 1024], replicated, may hold values from -0.1875 to 0.1875
- k_cache: bfloat16 [131072, 1024], P('hist', 'cand'), may hold values from -1.5 to 1.5
- v_cache: bfloat16 [131072, 1024], P('hist', 'cand'), may hold values from -6 to 6
- hist_len: int32 [16], replicated, may hold values from 1 to 32768, as said below
- cand_count: int32 [2, 16], replicated, may hold values from 1 to 128, 1024 in all within a row
- tile_user: int32 [1024], P('hist'), may hold values from 0 to 16, as said below
- tile_rank: int32 [1024], P('hist'), may hold values from 0 to 255, as said below
Outputs:
- ranked: bfloat16 [2, 1024, 1024], P(None, ('cand', 'hist'))
Inputs may be any that keep to these rules, and one draw needn't show every extreme that they name: A user's history fills exactly ceil(hist_len / 128) tile slots; one user's history is 32768 rows long. `tile_user`: slot owner, 16 for an empty slot; within each hist index's 128 slots the occupied ones come first; every user owns at least one slot. `tile_rank`: each tile position 0 to ceil(hist_len[u] / 128) - 1 of every user u stands in exactly one slot; empty slots hold 0. `cand_count`: row m gives the candidates of each user in micro-batch m, numbered user by user; they sum to 1024 and one user has exactly 128.
All inputs are finite; a program needn't handle non-finite values.
Results may differ from a plain program's by a relative error of at most 0.0051.
Values may be sent and summed in bfloat16 or wider, within the bound.
No kernel may reach another device: no remote copies, remote signals or barrier semaphores. Data moves between devices by JAX's collectives and lax.ppermute only.
A program may use at most 128 MiB of HBM per device.

v0:
```python
import jax
import jax.numpy as jnp
from jax import lax
from jax.sharding import PartitionSpec as P

HEAD_DIM = 128
TILE = 128
USERS = 16
MICRO = 2
EPSILON = 1e-06


def body(
    cand_x, qu_weight, out_weight, k_cache, v_cache, hist_len, cand_count, tile_user, tile_rank
):
    n_cand = lax.axis_size("cand")
    n_hist = lax.axis_size("hist")
    local_rows = cand_x.shape[1]
    model_width = cand_x.shape[2]
    head_cols = k_cache.shape[1]
    heads_here = head_cols // HEAD_DIM
    key_tiles = k_cache.reshape(-1, TILE, heads_here, HEAD_DIM)
    value_tiles = v_cache.reshape(-1, TILE, heads_here, HEAD_DIM)
    tiles_here = key_tiles.shape[0]
    per_turn = max(tiles_here // 8, 1)
    turn_count = tiles_here // per_turn
    user_ids = jnp.arange(USERS, dtype=jnp.int32)
    tile_rows = jnp.arange(TILE, dtype=jnp.int32)
    outputs = []
    for micro_index in range(MICRO):
        cand_rows = cand_x[micro_index]
        projected = jax.nn.silu(jnp.dot(cand_rows, qu_weight, preferred_element_type=jnp.float32))
        queries = projected[:, :model_width].astype(jnp.bfloat16)
        gate_vals = projected[:, model_width:].astype(jnp.bfloat16)
        gathered = lax.all_gather(queries, "hist", axis=0, tiled=True)
        queries_all = lax.all_to_all(gathered, "cand", split_axis=1, concat_axis=0, tiled=True)
        all_cands = queries_all.shape[0]
        window = 2 * all_cands // USERS
        counts = cand_count[micro_index]
        cand_start = jnp.cumsum(counts) - counts
        user_offsets = jnp.minimum(cand_start, all_cands - window)
        user_windows = jnp.stack(
            [
                lax.dynamic_slice_in_dim(queries_all, user_offsets[member], window, 0)
                for member in range(USERS)
            ]
        )
        row_ids = jnp.arange(window, dtype=jnp.int32)

        def visit_tiles(turn_index, user_sums):
            first_slot = turn_index * per_turn
            key_block = lax.dynamic_slice_in_dim(key_tiles, first_slot, per_turn, 0)
            value_block = lax.dynamic_slice_in_dim(value_tiles, first_slot, per_turn, 0)
            owners = lax.dynamic_slice_in_dim(tile_user, first_slot, per_turn, 0)
            positions = lax.dynamic_slice_in_dim(tile_rank, first_slot, per_turn, 0)
            matches = owners[:, None] == user_ids[None, :]
            length = jnp.sum(jnp.where(matches, hist_len[None, :], 0), axis=1)
            first_cand = jnp.sum(jnp.where(matches, cand_start[None, :], 0), axis=1)
            cand_total = jnp.sum(jnp.where(matches, counts[None, :], 0), axis=1)
            offsets = jnp.sum(jnp.where(matches, user_offsets[None, :], 0), axis=1)
            windows = jnp.einsum(
                "gu,uwc->gwc",
                matches.astype(jnp.bfloat16),
                user_windows,
                preferred_element_type=jnp.float32,
            ).astype(jnp.bfloat16)
            windows = windows.reshape(per_turn, window, heads_here, HEAD_DIM)
            scores = jnp.einsum(
                "gwhd,gkhd->ghwk", windows, key_block, preferred_element_type=jnp.float32
            )
            cand_ids = offsets[:, None] + row_ids[None, :]
            cand_ok = (cand_ids >= first_cand[:, None]) & (
                cand_ids < (first_cand + cand_total)[:, None]
            )
            key_ok = positions[:, None] * TILE + tile_rows[None, :] < length[:, None]
            keep_mask = cand_ok[:, None, :, None] & key_ok[:, None, None, :]
            weights = jnp.where(keep_mask, jax.nn.silu(scores), 0.0).astype(jnp.bfloat16)
            contrib = jnp.einsum(
                "ghwk,gkhd->gwhd", weights, value_block, preferred_element_type=jnp.float32
            )
            contrib = contrib.reshape(per_turn, window, head_cols)
            added = jnp.einsum(
                "gu,gwc->uwc", matches.astype(jnp.float32), contrib, precision=lax.Precision.HIGHEST
            )
            return user_sums + added

        user_sums = lax.fori_loop(
            0, turn_count, visit_tiles, jnp.zeros((USERS, window, head_cols), jnp.float32)
        )
        partial_value = jnp.zeros((all_cands, head_cols), jnp.float32)
        for member in range(USERS):
            current = lax.dynamic_slice_in_dim(partial_value, user_offsets[member], window, 0)
            partial_value = lax.dynamic_update_slice_in_dim(
                partial_value, current + user_sums[member], user_offsets[member], 0
            )
        blocks = partial_value.reshape(n_cand, n_hist, local_rows, head_cols)
        regrouped = lax.all_to_all(blocks, "cand", split_axis=0, concat_axis=3, tiled=True)
        attended = lax.psum_scatter(regrouped, "hist", scatter_dimension=1, tiled=True)
        attended = attended.reshape(local_rows, model_width)
        average = jnp.mean(attended, axis=-1, keepdims=True)
        centered = attended - average
        spread_sq = jnp.mean(centered * centered, axis=-1, keepdims=True)
        normed = centered * lax.rsqrt(spread_sq + EPSILON)
        mixed_rows = (normed * gate_vals.astype(jnp.float32)).astype(jnp.bfloat16)
        ranked = jnp.dot(
            mixed_rows, out_weight, preferred_element_type=jnp.float32
        ) + cand_rows.astype(jnp.float32)
        outputs.append(ranked.astype(jnp.bfloat16))
    return jnp.stack(outputs)


def solution(mesh):
    return jax.shard_map(
        body,
        mesh=mesh,
        in_specs=(
            P(None, ("cand", "hist"), None),
            P(),
            P(),
            P("hist", "cand"),
            P("hist", "cand"),
            P(),
            P(),
            P("hist"),
            P("hist"),
        ),
        out_specs=P(None, ("cand", "hist"), None),
        check_vma=False,
    )
```

profile of v0, /device:TPU:0, one launch (start us, length us, event | category | flops | bytes accessed | tf_op | source)
XLA Modules:
  0.0 606.1 jit_solution(5571507034580627950)
XLA Ops:
  9.8 16.7 %all_gather.6 = bf16[256,1024]{1,0:T(8,128)(2,1)S(1)} all-gather(bf16[32,1024]{1,0:T(8,128)(2,1)S(1)} %slice.354), channel_id=1, replica_groups=mesh['cand'=4,'hist'=8] {'hist'}, dimensions={0}, use_global_device_ids=true | all-gather | bytes 589824 | tf_op jit(solution)/shard_map/all_gather | solution.py:35
  76.7 12.5 %reshape.390 = bf16[128,128,2,128]{3,2,1,0:T(2,128)(2,1)} reshape(bf16[16384,256]{1,0:T(8,128)(2,1)} %param.17) | data formatting | bytes 16777216 | tf_op jit(solution)/shard_map/reshape | solution.py:23
  89.3 20.7 %copy.112 = bf16[128,128,2,128]{1,3,2,0:T(8,128)(2,1)} copy(bf16[128,128,2,128]{3,2,1,0:T(2,128)(2,1)} %reshape.390) | data formatting | bytes 16777216
  110.0 12.5 %reshape.391 = bf16[128,128,2,128]{3,2,1,0:T(2,128)(2,1)} reshape(bf16[16384,256]{1,0:T(8,128)(2,1)} %param.16) | data formatting | bytes 16777216 | tf_op jit(solution)/shard_map/reshape | solution.py:22
  122.5 9.1 %copy.114 = bf16[128,128,2,128]{3,1,2,0:T(8,128)(2,1)} copy(bf16[128,128,2,128]{3,2,1,0:T(2,128)(2,1)} %reshape.391) | data formatting | bytes 16777216
  131.7 14.8 %all_gather.7 = bf16[256,1024]{1,0:T(8,128)(2,1)S(1)} all-gather(bf16[32,1024]{1,0:T(8,128)(2,1)S(1)} %slice.372), channel_id=1, replica_groups=mesh['cand'=4,'hist'=8] {'hist'}, dimensions={0}, use_global_device_ids=true | all-gather | bytes 589824 | tf_op jit(solution)/shard_map/all_gather | solution.py:35
  173.6 129.4 %while.32 = (s32[]{:T(128)}, f32[16,128,256]{2,0,1:T(8,128)}, s32[128]{0:T(128)S(1)}, bf16[128,128,2,128]{1,3,2,0:T(8,128)(2,1)}, s32[16]{0:T(128)S(1)}, /*index...) while((s32[]{:T(128)}, f32[16,128,256]{2,0,1:T(8,128)}, ...), condition=%wide.region_6.7_spmd.clone.clone, body=%wide.region_1.6_spmd.clone.clone.sunk | while | flops 390871776 | bytes 20463428 | solution.py:87
  177.1 4.8 fusion.165
  192.8 4.8 fusion.165
  209.0 4.8 fusion.165
  241.6 4.8 fusion.165
  257.8 4.8 fusion.165
  290.3 4.8 fusion.165
  370.7 130.0 %while.33 = (s32[]{:T(128)}, f32[16,128,256]{2,0,1:T(8,128)}, s32[128]{0:T(128)S(1)}, bf16[128,128,2,128]{1,3,2,0:T(8,128)(2,1)}, s32[16]{0:T(128)S(1)}, /*index...) while((s32[]{:T(128)}, f32[16,128,256]{2,0,1:T(8,128)}, ...), condition=%wide.region_16.17_spmd.clone.clone, body=%wide.region_11.16_spmd.clone.clone.sunk | while | flops 390871776 | bytes 20467012 | solution.py:87
  374.2 4.8 fusion.175
  422.6 4.8 fusion.175
  430.5 4.8 select_add_fusion.5
  438.9 4.8 fusion.175
  446.9 4.8 select_add_fusion.5
  455.3 4.8 fusion.175
  463.2 4.8 select_add_fusion.5
  479.5 4.8 select_add_fusion.5
  537.2 18.7 %all_to_all.74 = f32[4,8,32,256]{3,2,1,0:T(8,128)S(1)} all-to-all(f32[4,8,32,256]{3,2,1,0:T(8,128)S(1)} %bitcast.340), channel_id=1, replica_groups=mesh['cand'=4,'hist'=8] {'cand'}, dimensions={0} | all-to-all | bytes 2097152 | tf_op jit(solution)/shard_map/all_to_all | solution.py:97
  563.5 30.9 %reduce-scatter.5.cloned.1.call-done = f32[1,1,32,1024]{3,2,1,0:T(8,128)} async-done(((f32[1,8,32,1024]{3,2,1,0:T(8,128)}), f32[1,1,32,1024]{3,2,1,0:T(8,128)}) %reduce-scatter.5.cloned.1.call-update) | async-done | bytes 131088 | tf_op jit(solution)/shard_map/reduce_scatter | solution.py:98
  (529 shorter events, 328.4 us)
Async XLA Ops:
  6.5 590.1 %copy-start = (bf16[1024,1024]{1,0:T(8,128)(2,1)S(1)}, bf16[1024,1024]{1,0:T(8,128)(2,1)}, u32[]{:S(2)}) copy-start(bf16[1024,1024]{1,0:T(8,128)(2,1)} %param.15) | copy-start | bytes 6291460
  9.8 17.6 %copy-start.5 = (bf16[32,2048]{1,0:T(8,128)(2,1)}, bf16[32,2048]{1,0:T(8,128)(2,1)S(1)}, u32[]{:S(2)}) copy-start(bf16[32,2048]{1,0:T(8,128)(2,1)S(1)} %multiply_convert_fusion.1) | copy-start | bytes 393220
  9.8 21.3 %copy-start.4 = (bf16[2,32,1024]{2,1,0:T(8,128)(2,1)S(1)}, bf16[2,32,1024]{2,1,0:T(8,128)(2,1)}, u32[]{:S(2)}) copy-start(bf16[2,32,1024]{2,1,0:T(8,128)(2,1)} %param.13) | copy-start | bytes 393220
  27.4 139.7 %all-to-all-start = ((bf16[256,4,256]{2,0,1:T(8,128)(2,1)}), bf16[256,4,256]{2,0,1:T(8,128)(2,1)S(1)}, u32[]{:S(2)}, u32[]{:S(2)}) async-start(bf16[256,4,256]{2,0,1:T(8,128)(2,1)} %bitcast.313), calls=%async_computation | async-start | bytes 1048576 | tf_op jit(solution)/shard_map/all_to_all | solution.py:36
  34.2 97.5 %copy-start.7 = (bf16[32,2048]{1,0:T(8,128)(2,1)}, bf16[32,2048]{1,0:T(8,128)(2,1)S(1)}, u32[]{:S(2)}) copy-start(bf16[32,2048]{1,0:T(8,128)(2,1)S(1)} %multiply_convert_fusion) | copy-start | bytes 393220
  167.0 182.9 %all-to-all-start.2 = ((bf16[256,4,256]{2,0,1:T(8,128)(2,1)}), bf16[256,4,256]{2,0,1:T(8,128)(2,1)}, u32[]{:S(2)}, u32[]{:S(2)}) async-start(bf16[256,4,256]{2,0,1:T(8,128)(2,1)} %bitcast.312), calls=%async_computation.3 | async-start | bytes 1048576 | tf_op jit(solution)/shard_map/all_to_all | solution.py:36
  349.9 174.8 %all-to-all-start.1 = ((f32[4,8,32,256]{3,2,1,0:T(8,128)}), f32[4,8,32,256]{3,2,1,0:T(8,128)}, u32[]{:S(2)}, u32[]{:S(2)}) async-start(f32[4,8,32,256]{3,2,1,0:T(8,128)} %bitcast.54), calls=%async_computation.1 | async-start | bytes 2097152 | tf_op jit(solution)/shard_map/all_to_all | solution.py:97
  354.2 207.2 %reduce-scatter.3.cloned.1.call-start = ((), (), s32[]{:S(2)}) async-start(), calls=%async_computation.6 | async-start | bytes 1179648 | tf_op jit(solution)/shard_map/reduce_scatter | solution.py:98
  354.5 16.2 %copy-start.10 = (s32[1,16]{1,0:T(1,128)S(1)}, s32[1,16]{1,0:T(1,128)}, u32[]{:S(2)}) copy-start(s32[1,16]{1,0:T(1,128)} %get-tuple-element.955) | copy-start | bytes 196
  354.5 16.2 %copy-start.14 = (s32[16]{0:T(128)S(1)}, s32[16]{0:T(128)}, u32[]{:S(2)}) copy-start(s32[16]{0:T(128)} %get-tuple-element.954) | copy-start | bytes 196
  397.9 4.8 copy-start.26
  414.2 4.8 copy-start.26
  430.5 4.8 copy-start.22
  430.5 4.8 copy-start.26
  446.9 4.8 copy-start.22
  446.9 4.8 copy-start.26
  463.2 4.8 copy-start.26
  479.5 4.8 copy-start.22
  479.5 4.8 copy-start.26
  495.9 4.8 copy-start.22
  495.9 4.8 copy-start.26
  527.1 67.3 %reduce-scatter.5.cloned.1.call-start = ((), (), s32[]{:S(2)}) async-start(), calls=%async_computation.7 | async-start | bytes 1179648 | tf_op jit(solution)/shard_map/reduce_scatter | solution.py:98
  555.8 40.8 %copy-start.6 = (bf16[32,2048]{1,0:T(8,128)(2,1)S(1)}, bf16[32,2048]{1,0:T(8,128)(2,1)}, u32[]{:S(2)}) copy-start(bf16[32,2048]{1,0:T(8,128)(2,1)} %copy-done.5) | copy-start | bytes 393220
  557.0 41.1 %copy-start.8 = (bf16[32,2048]{1,0:T(8,128)(2,1)S(1)}, bf16[32,2048]{1,0:T(8,128)(2,1)}, u32[]{:S(2)}) copy-start(bf16[32,2048]{1,0:T(8,128)(2,1)} %copy-done.7) | copy-start | bytes 393220
  (92 other events, 285.6 us)
Sparse Core Ops, SparseCore 0:
  527.3 34.0 reduce-scatter.2
  563.7 30.6 reduce-scatter.4
where the time goes:
time: 612 us; the launch traced here: 606 us
  local copies, waits for them, and re-layouts  203 us (33%)
  matrix products  186 us (30%)
  between operations  73.4 us (12%)
  blocking collectives  50.2 us (8%)
  other arithmetic  43.3 us (7%)
  waiting for transfers between devices  35.3 us (6%)
  starting transfers between devices  12.6 us (2%)
    dot_general x16, matrix products, visit_tiles(): jnp.einsum('ghwk,gkhd->gwhd', weights, value_block, preferred_element_typ...  76.4 us
    dot_general x16, matrix products, visit_tiles(): jnp.einsum('gu,gwc->uwc', matches.astype(jnp.float32), contrib, precision...  74.5 us
    reshape x16, local copies, waits for them, and re-layouts, visit_tiles(): contrib = contrib.reshape(per_turn, window, head_cols)  50.3 us
    unnamed x64, local copies, waits for them, and re-layouts  49.8 us
    dynamic_update_slice x32, local copies, waits for them, and re-layouts, body(): lax.dynamic_update_slice_in_dim(partial_value, current + user_sums[member...  42 us
    reduce_scatter x2, waiting for transfers between devices, body(): lax.psum_scatter(regrouped, 'hist', scatter_dimension=1, tiled=True)  35.2 us
    all_gather x2, blocking collectives, body(): gathered = lax.all_gather(queries, 'hist', axis=0, tiled=True)  31.5 us
    add x30, other arithmetic, body(): current + user_sums[member]  27.9 us
  transfers between devices with their start and end apart: 5, of which 2 were waited for; matrix products, arithmetic and copies ran while one was open for 69% of the time, Pallas kernels for 0%

commit v1 on v0

--- a/solution.py
+++ b/solution.py
@@ -32,7 +32,37 @@
         projected = jax.nn.silu(jnp.dot(cand_rows, qu_weight, preferred_element_type=jnp.float32))
         queries = projected[:, :model_width].astype(jnp.bfloat16)
         gate_vals = projected[:, model_width:].astype(jnp.bfloat16)
-        gathered = lax.all_gather(queries, "hist", axis=0, tiled=True)
+
+        def _write_windows(obj, a_name):
+            t_next, field_out, met_up = (
+                lax.axis_size(a_name),
+                lax.axis_index(a_name),
+                obj.shape[0],
+            )
+            items = [no * t_next if num == 0 else no for num, no in enumerate(obj.shape)]
+            mixed_arr = lax.dynamic_update_slice_in_dim(
+                jnp.zeros(items, obj.dtype), obj, field_out * met_up, axis=0
+            )
+            mid_arr = y1 = obj
+            ix = 1
+            while ix < t_next // 2 + 1:
+                mid_arr = lax.ppermute(
+                    mid_arr, a_name, [(num, (num + 1) % t_next) for num in range(t_next)]
+                )
+                mixed_arr = lax.dynamic_update_slice_in_dim(
+                    mixed_arr, mid_arr, (field_out - ix) % t_next * met_up, axis=0
+                )
+                if 2 * ix < t_next:
+                    y1 = lax.ppermute(
+                        y1, a_name, [(num, (num - 1) % t_next) for num in range(t_next)]
+                    )
+                    mixed_arr = lax.dynamic_update_slice_in_dim(
+                        mixed_arr, y1, (field_out + ix) % t_next * met_up, axis=0
+                    )
+                ix = ix + 1
+            return mixed_arr
+
+        gathered = _write_windows(queries, "hist")
         queries_all = lax.all_to_all(gathered, "cand", split_axis=1, concat_axis=0, tiled=True)
         all_cands = queries_all.shape[0]
         window = 2 * all_cands // USERS

time: 612 us -> 652 us (1.065)
  local copies, waits for them, and re-layouts: 203 us -> 252 us
  blocking collectives: 50.2 us -> 15 us
  starting transfers between devices: 12.6 us -> 33.3 us
  waiting for transfers between devices: 35.3 us -> 42.5 us
    dynamic_update_slice x0 -> x16, local copies, waits for them, and re-layouts: none -> 54.9 us  [the longest x8 25.1 us: _write_windows(): lax.dynamic_update_slice_in_dim(mixed_arr, mid_arr, (field_out - ix) % t_...]
    all_gather x2 -> x0, blocking collectives: 31.5 us -> none  [body(): gathered = lax.all_gather(queries, 'hist', axis=0, tiled=True)]
    ppermute x0 -> x14, starting transfers between devices: none -> 19.7 us  [the longest x6 18.6 us: _write_windows(): lax.ppermute(y1, a_name, [(num, (num - 1) % t_next) for num in range(t_ne...]
    unnamed x64 -> x66, local copies, waits for them, and re-layouts: 49.8 us -> 37.2 us
  transfers between devices with their start and end apart: 5 -> 19, of which waited for: 2 -> 4; matrix products, arithmetic and copies ran while one was open for 69% -> 72% of each run, Pallas kernels for 0% -> 0%
where the time goes in v1:
time: 652 us; the launch traced here: 647 us
  local copies, waits for them, and re-layouts  252 us (39%)
  matrix products  185 us (28%)
  between operations  74.3 us (11%)
  other arithmetic  43.4 us (7%)
  waiting for transfers between devices  42.5 us (7%)
  starting transfers between devices  33.3 us (5%)
  blocking collectives  15 us (2%)
    dot_general x16, matrix products, visit_tiles(): jnp.einsum('ghwk,gkhd->gwhd', weights, value_block, preferred_element_typ...  76.8 us
    dot_general x16, matrix products, visit_tiles(): jnp.einsum('gu,gwc->uwc', matches.astype(jnp.float32), contrib, precision...  74.6 us
    reshape x16, local copies, waits for them, and re-layouts, visit_tiles(): contrib = contrib.reshape(per_turn, window, head_cols)  50.3 us
    dynamic_update_slice x32, local copies, waits for them, and re-layouts, body(): lax.dynamic_update_slice_in_dim(partial_value, current + user_sums[member...  42.1 us
    reduce_scatter x2, waiting for transfers between devices, body(): lax.psum_scatter(regrouped, 'hist', scatter_dimension=1, tiled=True)  38.5 us
    unnamed x66, local copies, waits for them, and re-layouts  37.2 us
    add x30, other arithmetic, body(): current + user_sums[member]  27.9 us
    dot_general x16, matrix products, visit_tiles(): jnp.einsum('gu,uwc->gwc', matches.astype(jnp.bfloat16), user_windows, pre...  27.2 us
  transfers between devices with their start and end apart: 19, of which 4 were waited for; matrix products, arithmetic and copies ran while one was open for 72% of the time, Pallas kernels for 0%

profile of v1, /device:TPU:0, one launch (start us, length us, event | category | flops | bytes accessed | tf_op | source)
XLA Modules:
  0.0 646.5 jit_solution(7767348813571627145)
XLA Ops:
  112.6 12.5 %reshape.390 = bf16[128,128,2,128]{3,2,1,0:T(2,128)(2,1)} reshape(bf16[16384,256]{1,0:T(8,128)(2,1)} %param.17) | data formatting | bytes 16777216 | tf_op jit(solution)/shard_map/reshape | solution.py:23
  125.1 20.7 %copy.201 = bf16[128,128,2,128]{1,3,2,0:T(8,128)(2,1)} copy(bf16[128,128,2,128]{3,2,1,0:T(2,128)(2,1)} %reshape.390) | data formatting | bytes 16777216
  145.9 12.6 %reshape.391 = bf16[128,128,2,128]{3,2,1,0:T(2,128)(2,1)} reshape(bf16[16384,256]{1,0:T(8,128)(2,1)} %param.16) | data formatting | bytes 16777216 | tf_op jit(solution)/shard_map/reshape | solution.py:22
  158.5 9.2 %copy.203 = bf16[128,128,2,128]{3,1,2,0:T(8,128)(2,1)} copy(bf16[128,128,2,128]{3,2,1,0:T(2,128)(2,1)} %reshape.391) | data formatting | bytes 16777216
  223.9 131.1 %while.32 = (s32[]{:T(128)}, f32[16,128,256]{2,0,1:T(8,128)}, s32[128]{0:T(128)S(1)}, bf16[128,128,2,128]{1,3,2,0:T(8,128)(2,1)}, s32[16]{0:T(128)S(1)}, /*index...) while((s32[]{:T(128)}, f32[16,128,256]{2,0,1:T(8,128)}, ...), condition=%wide.region_6.7_spmd.clone.clone, body=%wide.region_1.6_spmd.clone.clone.sunk | while | flops 390871776 | bytes 20463428 | solution.py:117
  227.7 4.8 fusion.165
  243.5 4.8 fusion.165
  260.0 4.8 fusion.165
  276.4 4.8 fusion.165
  292.9 4.8 fusion.165
  309.4 4.8 fusion.165
  325.8 4.8 fusion.165
  342.3 4.8 fusion.165
  410.0 131.5 %while.33 = (s32[]{:T(128)}, f32[16,128,256]{2,0,1:T(8,128)}, s32[128]{0:T(128)S(1)}, bf16[128,128,2,128]{1,3,2,0:T(8,128)(2,1)}, s32[16]{0:T(128)S(1)}, /*index...) while((s32[]{:T(128)}, f32[16,128,256]{2,0,1:T(8,128)}, ...), condition=%wide.region_16.17_spmd.clone.clone, body=%wide.region_11.16_spmd.clone.clone.sunk | while | flops 390871776 | bytes 20467012 | solution.py:117
  413.8 4.8 fusion.175
  446.2 4.8 fusion.175
  462.7 4.8 fusion.175
  479.2 4.8 fusion.175
  495.7 4.8 fusion.175
  512.2 4.8 fusion.175
  528.8 4.8 fusion.175
  578.0 15.0 %all_to_all.74 = f32[4,8,32,256]{3,2,1,0:T(8,128)S(1)} all-to-all(f32[4,8,32,256]{3,2,1,0:T(8,128)S(1)} %bitcast.332), channel_id=1, replica_groups=mesh['cand'=4,'hist'=8] {'cand'}, dimensions={0} | all-to-all | bytes 2097152 | tf_op jit(solution)/shard_map/all_to_all | solution.py:127
  594.2 7.8 %reduce-scatter.3.cloned.1.call-done = f32[1,1,32,1024]{3,2,1,0:T(8,128)} async-done(((f32[1,8,32,1024]{3,2,1,0:T(8,128)}), f32[1,1,32,1024]{3,2,1,0:T(8,128)}) %reduce-scatter.3.cloned.1.call-update) | async-done | bytes 131088 | tf_op jit(solution)/shard_map/reduce_scatter | solution.py:128
  604.1 30.7 %reduce-scatter.5.cloned.1.call-done = f32[1,1,32,1024]{3,2,1,0:T(8,128)} async-done(((f32[1,8,32,1024]{3,2,1,0:T(8,128)}), f32[1,1,32,1024]{3,2,1,0:T(8,128)}) %reduce-scatter.5.cloned.1.call-update) | async-done | bytes 131088 | tf_op jit(solution)/shard_map/reduce_scatter | solution.py:128
  (591 shorter events, 390.3 us)
Async XLA Ops:
  6.5 630.5 %copy-start = (bf16[1024,1024]{1,0:T(8,128)(2,1)S(1)}, bf16[1024,1024]{1,0:T(8,128)(2,1)}, u32[]{:S(2)}) copy-start(bf16[1024,1024]{1,0:T(8,128)(2,1)} %param.15) | copy-start | bytes 6291460
  6.5 15.4 %copy-start.1 = (bf16[1024,2048]{1,0:T(8,128)(2,1)S(1)}, bf16[1024,2048]{1,0:T(8,128)(2,1)}, u32[]{:S(2)}) copy-start(bf16[1024,2048]{1,0:T(8,128)(2,1)} %param.14) | copy-start | bytes 12582916
  9.8 17.7 %copy-start.19 = (s32[2,16]{1,0:T(2,128)S(1)}, s32[2,16]{1,0:T(2,128)}, u32[]{:S(2)}) copy-start(s32[2,16]{1,0:T(2,128)} %param.19) | copy-start | bytes 388
  9.8 6.5 %collective-permute-start = (bf16[32,1024]{1,0:T(8,128)(2,1)S(1)}, bf16[32,1024]{1,0:T(8,128)(2,1)S(1)}, u32[]{:S(2)}, u32[]{:S(2)}) collective-permute-start(bf16[32,1024]{1,0:T(8,128)(2,1)S(1)} %slice.354), channel_id=1, source_target_pairs={{0,1},{1,2},{2,3},{3,4},{4,5},{5,6},{6,7},{7,0},{8,9},{9,10},{10,1... | collective-permute-start | bytes 196616 | tf_op jit(solution)/shard_map/ppermute | solution.py:49
  10.3 6.0 collective-permute-start.1
  16.3 5.6 collective-permute-start.2
  16.3 10.7 %collective-permute-start.3 = (bf16[32,1024]{1,0:T(8,128)(2,1)S(1)}, bf16[32,1024]{1,0:T(8,128)(2,1)S(1)}, u32[]{:S(2)}, u32[]{:S(2)}) collective-permute-start(bf16[32,1024]{1,0:T(8,128)(2,1)S(1)} %collective-permute-done.1), channel_id=1, source_target_pairs={{0,7},{1,0},{2,1},{3,2},{4,3},{5,4},{6,5},{7,6},{8,15},{9,8},{10,9... | collective-permute-start | bytes 196616 | tf_op jit(solution)/shard_map/ppermute | solution.py:56
  21.9 5.6 collective-permute-start.4
  23.4 17.1 %collective-permute-start.7 = (bf16[32,1024]{1,0:T(8,128)(2,1)S(1)}, bf16[32,1024]{1,0:T(8,128)(2,1)S(1)}, u32[]{:S(2)}, u32[]{:S(2)}) collective-permute-start(bf16[32,1024]{1,0:T(8,128)(2,1)S(1)} %slice.372), channel_id=1, source_target_pairs={{0,1},{1,2},{2,3},{3,4},{4,5},{5,6},{6,7},{7,0},{8,9},{9,10},{10,1... | collective-permute-start | bytes 196616 | tf_op jit(solution)/shard_map/ppermute | solution.py:49
  23.4 40.7 %collective-permute-start.8 = (bf16[32,1024]{1,0:T(8,128)(2,1)S(1)}, bf16[32,1024]{1,0:T(8,128)(2,1)S(1)}, u32[]{:S(2)}, u32[]{:S(2)}) collective-permute-start(bf16[32,1024]{1,0:T(8,128)(2,1)S(1)} %slice.372), channel_id=1, source_target_pairs={{0,7},{1,0},{2,1},{3,2},{4,3},{5,4},{6,5},{7,6},{8,15},{9,8},{10,9... | collective-permute-start | bytes 196616 | tf_op jit(solution)/shard_map/ppermute | solution.py:56
  27.0 25.0 %collective-permute-start.5 = (bf16[32,1024]{1,0:T(8,128)(2,1)S(1)}, bf16[32,1024]{1,0:T(8,128)(2,1)S(1)}, u32[]{:S(2)}, u32[]{:S(2)}) collective-permute-start(bf16[32,1024]{1,0:T(8,128)(2,1)S(1)} %collective-permute-done.3), channel_id=1, source_target_pairs={{0,7},{1,0},{2,1},{3,2},{4,3},{5,4},{6,5},{7,6},{8,15},{9,8},{10,9... | collective-permute-start | bytes 196616 | tf_op jit(solution)/shard_map/ppermute | solution.py:56
  27.5 28.4 %collective-permute-start.6 = (bf16[32,1024]{1,0:T(8,128)(2,1)S(1)}, bf16[32,1024]{1,0:T(8,128)(2,1)S(1)}, u32[]{:S(2)}, u32[]{:S(2)}) collective-permute-start(bf16[32,1024]{1,0:T(8,128)(2,1)S(1)} %collective-permute-done.4), channel_id=1, source_target_pairs={{0,1},{1,2},{2,3},{3,4},{4,5},{5,6},{6,7},{7,0},{8,9},{9,10},{10,1... | collective-permute-start | bytes 196616 | tf_op jit(solution)/shard_map/ppermute | solution.py:49
  40.6 26.9 %collective-permute-start.9 = (bf16[32,1024]{1,0:T(8,128)(2,1)S(1)}, bf16[32,1024]{1,0:T(8,128)(2,1)S(1)}, u32[]{:S(2)}, u32[]{:S(2)}) collective-permute-start(bf16[32,1024]{1,0:T(8,128)(2,1)S(1)} %collective-permute-done.7), channel_id=1, source_target_pairs={{0,1},{1,2},{2,3},{3,4},{4,5},{5,6},{6,7},{7,0},{8,9},{9,10},{10,1... | collective-permute-start | bytes 196616 | tf_op jit(solution)/shard_map/ppermute | solution.py:49
  59.0 158.2 %all-to-all-start = ((bf16[256,4,256]{0,2,1:T(8,128)(2,1)}), bf16[256,4,256]{0,2,1:T(8,128)(2,1)S(1)}, u32[]{:S(2)}, u32[]{:S(2)}) async-start(bf16[256,4,256]{0,2,1:T(8,128)(2,1)} %bitcast.3), calls=%async_computation | async-start | bytes 1048576 | tf_op jit(solution)/shard_map/all_to_all | solution.py:66
  64.2 24.6 %collective-permute-start.10 = (bf16[32,1024]{1,0:T(8,128)(2,1)S(1)}, bf16[32,1024]{1,0:T(8,128)(2,1)S(1)}, u32[]{:S(2)}, u32[]{:S(2)}) collective-permute-start(bf16[32,1024]{1,0:T(8,128)(2,1)S(1)} %collective-permute-done.8), channel_id=1, source_target_pairs={{0,7},{1,0},{2,1},{3,2},{4,3},{5,4},{6,5},{7,6},{8,15},{9,8},{10,9... | collective-permute-start | bytes 196616 | tf_op jit(solution)/shard_map/ppermute | solution.py:56
  67.4 24.9 %collective-permute-start.11 = (bf16[32,1024]{1,0:T(8,128)(2,1)S(1)}, bf16[32,1024]{1,0:T(8,128)(2,1)S(1)}, u32[]{:S(2)}, u32[]{:S(2)}) collective-permute-start(bf16[32,1024]{1,0:T(8,128)(2,1)S(1)} %collective-permute-done.9), channel_id=1, source_target_pairs={{0,1},{1,2},{2,3},{3,4},{4,5},{5,6},{6,7},{7,0},{8,9},{9,10},{10,1... | collective-permute-start | bytes 196616 | tf_op jit(solution)/shard_map/ppermute | solution.py:49
  88.7 121.4 %collective-permute-start.12 = (bf16[32,1024]{1,0:T(8,128)(2,1)S(1)}, bf16[32,1024]{1,0:T(8,128)(2,1)S(1)}, u32[]{:S(2)}, u32[]{:S(2)}) collective-permute-start(bf16[32,1024]{1,0:T(8,128)(2,1)S(1)} %collective-permute-done.10), channel_id=1, source_target_pairs={{0,7},{1,0},{2,1},{3,2},{4,3},{5,4},{6,5},{7,6},{8,15},{9,8},{10,9... | collective-permute-start | bytes 196616 | tf_op jit(solution)/shard_map/ppermute | solution.py:56
  92.3 121.9 %collective-permute-start.13 = (bf16[32,1024]{1,0:T(8,128)(2,1)S(1)}, bf16[32,1024]{1,0:T(8,128)(2,1)S(1)}, u32[]{:S(2)}, u32[]{:S(2)}) collective-permute-start(bf16[32,1024]{1,0:T(8,128)(2,1)S(1)} %collective-permute-done.11), channel_id=1, source_target_pairs={{0,1},{1,2},{2,3},{3,4},{4,5},{5,6},{6,7},{7,0},{8,9},{9,10},{10,1... | collective-permute-start | bytes 196616 | tf_op jit(solution)/shard_map/ppermute | solution.py:49
  217.2 184.8 %all-to-all-start.2 = ((bf16[256,4,256]{0,2,1:T(8,128)(2,1)}), bf16[256,4,256]{0,2,1:T(8,128)(2,1)}, u32[]{:S(2)}, u32[]{:S(2)}) async-start(bf16[256,4,256]{0,2,1:T(8,128)(2,1)} %bitcast.62), calls=%async_computation.3 | async-start | bytes 1048576 | tf_op jit(solution)/shard_map/all_to_all | solution.py:66
  402.0 163.5 %all-to-all-start.1 = ((f32[4,8,32,256]{3,2,1,0:T(8,128)}), f32[4,8,32,256]{3,2,1,0:T(8,128)}, u32[]{:S(2)}, u32[]{:S(2)}) async-start(f32[4,8,32,256]{3,2,1,0:T(8,128)} %bitcast.54), calls=%async_computation.1 | async-start | bytes 2097152 | tf_op jit(solution)/shard_map/all_to_all | solution.py:127
  406.2 195.7 %reduce-scatter.3.cloned.1.call-start = ((), (), s32[]{:S(2)}) async-start(), calls=%async_computation.6 | async-start | bytes 1179648 | tf_op jit(solution)/shard_map/reduce_scatter | solution.py:128
  567.9 66.9 %reduce-scatter.5.cloned.1.call-start = ((), (), s32[]{:S(2)}) async-start(), calls=%async_computation.7 | async-start | bytes 1179648 | tf_op jit(solution)/shard_map/reduce_scatter | solution.py:128
  593.0 44.0 %copy-start.7 = (bf16[32,2048]{1,0:T(8,128)(2,1)S(1)}, bf16[32,2048]{1,0:T(8,128)(2,1)}, u32[]{:S(2)}) copy-start(bf16[32,2048]{1,0:T(8,128)(2,1)} %copy-done.6) | copy-start | bytes 393220
  594.1 44.3 %copy-start.9 = (bf16[32,2048]{1,0:T(8,128)(2,1)S(1)}, bf16[32,2048]{1,0:T(8,128)(2,1)}, u32[]{:S(2)}) copy-start(bf16[32,2048]{1,0:T(8,128)(2,1)} %copy-done.8) | copy-start | bytes 393220
  (107 other events, 363.6 us)
Sparse Core Ops, SparseCore 0:
  568.1 33.8 reduce-scatter.2
  604.2 30.5 reduce-scatter.4
